TPU v7x, 128 devices: a whole 4x4x4 slice. The times are simulated.
128 devices in a mesh: dp: 32 (over y, x, core), tensor: 4 (over z).
Axes of the slice: x: 4, y: 4, z: 4, core: 2. Of those that a mesh axis runs over, the one named last changes fastest.
Arguments:
- layer_input: bfloat16 [4096, 2560], P('dp'), may hold values from -6 to 6
- inner_out: bfloat16 [4096, 2560], P('dp', 'tensor'), may hold values from -6 to 6
- out_grad: bfloat16 [4096, 2560], P('dp'), may hold values from -0.09375 to 0.09375
- zx_grad: bfloat16 [4096, 5120], P('dp', 'tensor'), may hold values from -0.09375 to 0.09375
- bc_grad: bfloat16 [4096, 1024], P('dp', 'tensor'), may hold values from -0.09375 to 0.09375
- dt_grad: bfloat16 [4096, 40], P('dp', 'tensor'), may hold values from -0.09375 to 0.09375
- owner_deal: int32 [4, 31], P('tensor'), may hold values from 0 to 31, as said below
- head_momentum: float32 [4, 2368, 2560], P('tensor', 'dp'), may hold values from -6 to 6
- bc_momentum: float32 [2, 128, 2560], replicated, may hold values from -6 to 6
Outputs:
- head_update: bfloat16 [40, 3, 64, 2560], P('tensor')
- dt_update: bfloat16 [40, 2560], P('tensor')
- bc_update: bfloat16 [2, 128, 2560], replicated
- head_momentum_out: float32 [4, 2368, 2560], P('tensor', 'dp')
- bc_momentum_out: float32 [2, 128, 2560], replicated
Inputs may be any that keep to these rules, and one draw needn't show every extreme that they name: `owner_deal`: each owner holds at most 1 head blocks of one tensor index; the owner of the dt block (the last entry) holds exactly 1 head blocks of that index as well, so it holds exactly 74 rows.
All inputs are finite; a program needn't handle non-finite values.
Results may differ from a plain program's by a relative error of at most 0.0085.
Values may be sent and summed in bfloat16 or wider, within the bound.
No kernel may reach another device: no remote copies, remote signals or barrier semaphores. Data moves between devices by JAX's collectives and lax.ppermute only.
A program may use at most 128 MiB of HBM per device.

v0:
```python
import math
import jax
import jax.numpy as jnp
from jax import lax
from jax.sharding import PartitionSpec as P

HD = 64
STATE = 128
NS_ITERS = 5
quintic_first = 3.4445
quintic_second = -4.775
quintic_third = 2.0315
momentum_decay = 0.95
norm_epsilon = 1e-07


def orthogonalize(moment):
    highest = lax.Precision.HIGHEST
    norm_value = jnp.sqrt(jnp.sum(moment * moment, axis=(1, 2), keepdims=True))
    current = moment / (norm_value + norm_epsilon)
    for step in range(NS_ITERS):
        gram_matrix = jnp.einsum("bik,bjk->bij", current, current, precision=highest)
        polynomial = quintic_second * gram_matrix + quintic_third * jnp.einsum(
            "bij,bjk->bik", gram_matrix, gram_matrix, precision=highest
        )
        current = quintic_first * current + jnp.einsum(
            "bij,bjk->bik", polynomial, current, precision=highest
        )
    return current


def on_device(
    layer_input,
    inner_out,
    out_grad,
    zx_grad,
    bc_grad,
    dt_grad,
    owner_deal,
    head_momentum,
    bc_momentum,
):
    n_data = lax.axis_size("dp")
    tokens, width = layer_input.shape
    heads_here = dt_grad.shape[1]
    capacity = head_momentum.shape[1]
    n_blocks = 3 * heads_here
    contract = (((0,), (0,)), ((), ()))
    f32, bf16 = (jnp.float32, jnp.bfloat16)
    owners = owner_deal[0]
    head_owner = owners[:n_blocks]
    dt_owner = owners[n_blocks]
    slots = jnp.arange(n_data, dtype=jnp.int32)
    bc_cols = jnp.sum(lax.all_gather(bc_grad, "tensor", axis=0).astype(f32), axis=0)
    bc_part = lax.dot_general(
        bc_cols,
        layer_input.astype(f32),
        contract,
        precision=lax.Precision.HIGHEST,
        preferred_element_type=f32,
    )
    bc_summed = lax.psum(bc_part, "dp")
    zx = zx_grad.reshape(tokens, heads_here, 2, HD)
    io = inner_out.reshape(tokens, heads_here, 1, HD)
    upper = jnp.concatenate([zx, jnp.zeros_like(io)], axis=2).reshape(tokens, n_blocks, HD)
    lower = jnp.concatenate([jnp.zeros_like(zx), io], axis=2).reshape(tokens, n_blocks, HD)
    grad_blocks = jnp.concatenate([upper, lower], axis=0)
    pick = (head_owner[None, :] == slots[:, None]).astype(bf16)
    owner_cols = jnp.einsum("tbr,ob->tor", grad_blocks, pick, preferred_element_type=f32).astype(
        bf16
    )
    dt_cols = jnp.concatenate([dt_grad, jnp.zeros_like(dt_grad)], axis=0)
    is_dt = (slots == dt_owner).astype(bf16)
    dt_owner_cols = dt_cols[:, None, :] * is_dt[None, :, None]
    chunk = -(-capacity // 16) * 16
    pad_cols = jnp.zeros((2 * tokens, n_data, chunk - capacity), bf16)
    send_cols = jnp.concatenate([owner_cols, dt_owner_cols, pad_cols], axis=2).reshape(
        2 * tokens, n_data * chunk
    )
    factors = jnp.concatenate([layer_input, out_grad], axis=0)
    send = lax.dot_general(send_cols, factors, contract, preferred_element_type=f32).astype(bf16)
    owned_sum = lax.psum_scatter(send, "dp", scatter_dimension=0, tiled=True)[:capacity].astype(f32)
    moment = momentum_decay * head_momentum[0] + owned_sum
    head_direction = orthogonalize(moment[None, :HD])[0]
    dt_direction = orthogonalize(moment[None, HD:])[0]
    head_gathered = lax.all_gather(
        (head_direction * math.sqrt(width)).astype(bf16), "dp", axis=0, tiled=False
    )
    tail = jnp.concatenate([dt_direction, jnp.zeros((chunk - capacity, width), f32)], axis=0)
    tail_gathered = lax.all_gather(
        (tail * math.sqrt(width)).astype(bf16), "dp", axis=0, tiled=False
    )
    head_update = jnp.take(head_gathered, head_owner, axis=0, mode="clip").reshape(
        heads_here, 3, HD, width
    )
    dt_update = lax.dynamic_slice(tail_gathered, (dt_owner, 0, 0), (1, heads_here, width))[0]
    bc_moment = momentum_decay * bc_momentum + bc_summed.reshape(2, STATE, width)
    bc_update = (orthogonalize(bc_moment) * math.sqrt(width)).astype(bf16)
    return (head_update, dt_update, bc_update, moment[None], bc_moment)


def solution(mesh):
    in_specs = (
        P("dp", None),
        P("dp", "tensor"),
        P("dp", None),
        P("dp", "tensor"),
        P("dp", "tensor"),
        P("dp", "tensor"),
        P("tensor", None),
        P("tensor", "dp", None),
        P(),
    )
    out_specs = (
        P("tensor", None, None, None),
        P("tensor", None),
        P(),
        P("tensor", "dp", None),
        P(),
    )
    return jax.shard_map(
        on_device, mesh=mesh, in_specs=in_specs, out_specs=out_specs, check_vma=False
    )
```

profile of v0, /device:TPU:1, one launch (start us, length us, event | category | flops | bytes accessed | tf_op | source)
XLA Modules:
  0.0 366.2 jit_solution(17709010283561353093)
XLA Ops:
  7.2 1.2 slice.18
  9.8 1.1 copy.20
  10.8 0.7 concatenate.24
  12.0 1.2 copy.19
  14.4 0.7 copy.24
  15.4 6.7 %convolution_convert_fusion = bf16[2560,2560]{1,0:T(8,128)(2,1)} fusion(bf16[256,2560]{0,1:T(8,128)(2,1)S(1)} %bitcast.114, bf16[128,2560]{1,0:T(8,128)(2,1)S(1)} %copy-done.4, bf16[128,2560]{1,0:T(8,128)(2,1)S(1)} %copy-done), kind=kOutput, calls=%fused_computation.1 | convolution fusion | flops 3364618240 | bytes 15728640 | tf_op jit(solution)/shard_map/dot_general | solution.py:81
  22.2 0.8 copy-done.5
  23.0 12.3 %all-gather.2 = bf16[512,256]{1,0:T(8,128)(2,1)S(1)} all-gather(bf16[128,256]{1,0:T(8,128)(2,1)S(1)} %copy-done.5), channel_id=4, replica_groups=mesh['dp'=32,'tensor'=4] {'tensor'}, dimensions={0}, use_global_device_ids=true | all-gather | bytes 327680 | tf_op jit(solution)/shard_map/all_gather | solution.py:54
  35.3 2.7 fusion.42
  38.1 91.4 %reduce-scatter.2.cloned.1.call-done = bf16[80,2560]{1,0:T(8,128)(2,1)} async-done(((bf16[2560,2560]{1,0:T(8,128)(2,1)}), bf16[80,2560]{1,0:T(8,128)(2,1)}) %reduce-scatter.2.cloned.1.call-update) | async-done | bytes 409616 | tf_op jit(solution)/shard_map/reduce_scatter | solution.py:82
  129.5 1.1 bitcast_add_fusion
  137.0 0.8 multiply_reduce_fusion.1
  139.3 0.7 convolution_add_fusion.9
  140.9 0.7 convolution_add_fusion.8
  145.5 1.4 fusion.3
  148.9 93.6 %all-reduce.6.cloned.1.call-done = f32[2,128,2560]{2,1,0:T(8,128)} async-done(((f32[2,128,2560]{2,1,0:T(8,128)}), f32[2,128,2560]{2,1,0:T(8,128)}) %all-reduce.6.cloned.1.call-update) | async-done | bytes 2621456 | tf_op jit(solution)/shard_map/psum | solution.py:62
  242.5 2.3 multiply_reduce_fusion
  244.8 2.8 fusion.26
  247.9 2.8 convolution_add_fusion.4
  250.7 2.5 fusion.43
  253.5 2.6 convolution_add_fusion.3
  256.2 2.5 fusion.44
  259.0 2.6 convolution_add_fusion.2
  261.6 2.7 fusion.45
  264.6 2.6 convolution_add_fusion.1
  267.3 2.5 fusion.46
  270.1 3.7 %fusion.1 = bf16[2,128,2560]{2,1,0:T(8,128)(2,1)} fusion(f32[2,128,128]{2,1,0:T(8,128)S(1)} %fusion.8, f32[2,128,2560]{2,1,0:T(8,128)S(1)} %convolution_add_fusion.1), kind=kOutput, calls=%fused_computation.8 | convolution fusion | flops 1009254400 | bytes 4063232 | tf_op jit(solution)/shard_map/bij,bjk->bik/dot_general | solution.py:26
  273.8 1.6 copy.25
  275.4 14.4 %all-gather.8.cloned.1.call-done = bf16[512,2560]{1,0:T(8,128)(2,1)} async-done(((bf16[16,2560]{1,0:T(8,128)(2,1)}), bf16[512,2560]{1,0:T(8,128)(2,1)}) %all-gather.8.cloned.1.call-update) | async-done | bytes 2621456 | tf_op jit(solution)/shard_map/all_gather | solution.py:90
  289.8 1.5 dynamic-slice_bitcast_fusion
  291.4 58.2 %all-gather.6.cloned.1.call-done = bf16[2048,2560]{1,0:T(8,128)(2,1)} async-done(((bf16[64,2560]{1,0:T(8,128)(2,1)}), bf16[2048,2560]{1,0:T(8,128)(2,1)}) %all-gather.6.cloned.1.call-update) | async-done | bytes 10485776 | tf_op jit(solution)/shard_map/all_gather | solution.py:86
  349.5 9.9 %gather_fusion = bf16[30,64,2560]{2,1,0:T(8,128)(2,1)} fusion(bf16[32,64,2560]{2,1,0:T(8,128)(2,1)} %bitcast.112, s32[1024]{0:T(1024)S(1)} %pad_clamp_fusion), kind=kCustom, calls=%fused_computation | custom fusion | bytes 19660920 | tf_op jit(solution)/shard_map/jit(_take)/gather | solution.py:93
  (67 shorter events, 15.9 us)
Async XLA Ops:
  7.2 122.4 %reduce-scatter.2.cloned.1.call-start = ((), (), s32[]{:S(2)}) async-start(), calls=%async_computation.1 | async-start | bytes 13516800 | tf_op jit(solution)/shard_map/reduce_scatter | solution.py:82
  14.1 1.1 copy-start
  14.1 1.3 copy-start.4
  22.1 0.8 copy-start.5
  22.2 220.3 %all-reduce.6.cloned.1.call-start = ((), (), s32[]{:S(2)}) async-start(), calls=%async_computation.2 | async-start | bytes 5242880 | tf_op jit(solution)/shard_map/psum | solution.py:62
  35.3 94.2 %copy-start.3 = (f32[1,74,2560]{2,0,1:T(1,128)S(1)}, f32[1,74,2560]{2,0,1:T(1,128)}, u32[]{:S(2)}) copy-start(f32[1,74,2560]{2,0,1:T(1,128)} %param.16) | copy-start | bytes 2273284
  38.1 251.8 %all-gather.8.cloned.1.call-start = ((), (), s32[]{:S(2)}) async-start(), calls=%async_computation.4 | async-start | bytes 2703360 | tf_op jit(solution)/shard_map/all_gather | solution.py:90
  136.5 213.0 %all-gather.6.cloned.1.call-start = ((), (), s32[]{:S(2)}) async-start(), calls=%async_computation.3 | async-start | bytes 10813440 | tf_op jit(solution)/shard_map/all_gather | solution.py:86
  143.1 99.4 %copy-start.1 = (f32[2,128,2560]{2,1,0:T(8,128)S(1)}, f32[2,128,2560]{2,1,0:T(8,128)}, u32[]{:S(2)}) copy-start(f32[2,128,2560]{2,1,0:T(8,128)} %param.17) | copy-start | bytes 7864324
  244.8 3.1 copy-start.2
Sparse Core Ops, SparseCore 0:
  22.3 107.2 reduce-scatter.1
  133.4 109.0 all-reduce.5
  245.3 44.4 all-gather.7
  292.5 56.9 all-gather.5
where the time goes:
time: 372 us; the launch traced here: 366 us
  waiting for transfers between devices  258 us (69%)
  matrix products  50.8 us (14%)
  local copies, waits for them, and re-layouts  20.6 us (6%)
  between operations  17.7 us (5%)
  blocking collectives  12.3 us (3%)
  other arithmetic  6.46 us (2%)
    psum x1, waiting for transfers between devices, on_device(): bc_summed = lax.psum(bc_part, 'dp')  93.6 us
    reduce_scatter x1, waiting for transfers between devices, on_device(): lax.psum_scatter(send, 'dp', scatter_dimension=0, tiled=True)[:capacity]  91.4 us
    all_gather x1, waiting for transfers between devices, on_device(): lax.all_gather((head_direction * math.sqrt(width)).astype(bf16), 'dp', ax...  58.2 us
    dot_general x15, matrix products, orthogonalize(): jnp.einsum('bij,bjk->bik', polynomial, current, precision=highest)  20.1 us
    dot_general x15, matrix products, orthogonalize(): jnp.einsum('bik,bjk->bij', current, current, precision=highest)  17.7 us
    all_gather x1, waiting for transfers between devices, on_device(): lax.all_gather((tail * math.sqrt(width)).astype(bf16), 'dp', axis=0, tile...  14.4 us
    all_gather x1, blocking collectives, on_device(): lax.all_gather(bc_grad, 'tensor', axis=0).astype(f32)  12.3 us
    gather x1, local copies, waits for them, and re-layouts, on_device(): jnp.take(head_gathered, head_owner, axis=0, mode='clip')  9.86 us
  transfers between devices with their start and end apart: 4, of which 4 were waited for; matrix products, arithmetic and copies ran while one was open for 14% of the time, Pallas kernels for 0%

commit v1 on v0

--- a/solution.py
+++ b/solution.py
@@ -59,7 +59,11 @@
         precision=lax.Precision.HIGHEST,
         preferred_element_type=f32,
     )
-    bc_summed = lax.psum(bc_part, "dp")
+    bc_summed = bc_part
+    for hop in (1, 2, 4, 8, 16):
+        bc_summed = bc_summed + lax.ppermute(
+            bc_summed, "dp", [(dev, dev ^ hop) for dev in range(32)]
+        )
     zx = zx_grad.reshape(tokens, heads_here, 2, HD)
     io = inner_out.reshape(tokens, heads_here, 1, HD)
     upper = jnp.concatenate([zx, jnp.zeros_like(io)], axis=2).reshape(tokens, n_blocks, HD)

time: 372 us -> 490 us (1.32)
  waiting for transfers between devices: 258 us -> 364 us
  starting transfers between devices: 0.63 us -> 12.6 us
    ppermute x0 -> x5, waiting for transfers between devices: none -> 257 us  [on_device(): lax.ppermute(bc_summed, 'dp', [(dev, dev ^ hop) for dev in range(32)])]
    psum x1 -> x0, waiting for transfers between devices: 93.6 us -> none  [on_device(): bc_summed = lax.psum(bc_part, 'dp')]
    all_gather x1, waiting for transfers between devices: 58.2 us -> 0.01 us  [on_device(): lax.all_gather((head_direction * math.sqrt(width)).astype(bf16), 'dp', ax...]
    reduce_scatter x1, waiting for transfers between devices: 91.4 us -> 107 us  [on_device(): lax.psum_scatter(send, 'dp', scatter_dimension=0, tiled=True)[:capacity]]
    all_gather x1, waiting for transfers between devices: 14.4 us -> 0.01 us  [on_device(): lax.all_gather((tail * math.sqrt(width)).astype(bf16), 'dp', axis=0, tile...]
    ppermute x0 -> x5, starting transfers between devices: none -> 11.9 us  [on_device(): lax.ppermute(bc_summed, 'dp', [(dev, dev ^ hop) for dev in range(32)])]
  transfers between devices with their start and end apart: 4 -> 8, of which waited for: 4 -> 6; matrix products, arithmetic and copies ran while one was open for 14% -> 10% of each run, Pallas kernels for 0% -> 0%
where the time goes in v1:
time: 490 us; the launch traced here: 483 us
  waiting for transfers between devices  364 us (74%)
  matrix products  50.1 us (10%)
  local copies, waits for them, and re-layouts  19.9 us (4%)
  between operations  17.8 us (4%)
  starting transfers between devices  12.6 us (3%)
  blocking collectives  10.7 us (2%)
  other arithmetic  8.12 us (2%)
    ppermute x5, waiting for transfers between devices, on_device(): lax.ppermute(bc_summed, 'dp', [(dev, dev ^ hop) for dev in range(32)])  257 us
    reduce_scatter x1, waiting for transfers between devices, on_device(): lax.psum_scatter(send, 'dp', scatter_dimension=0, tiled=True)[:capacity]  107 us
    dot_general x15, matrix products, orthogonalize(): jnp.einsum('bij,bjk->bik', polynomial, current, precision=highest)  20.2 us
    dot_general x15, matrix products, orthogonalize(): jnp.einsum('bik,bjk->bij', current, current, precision=highest)  18.5 us
    ppermute x5, starting transfers between devices, on_device(): lax.ppermute(bc_summed, 'dp', [(dev, dev ^ hop) for dev in range(32)])  11.9 us
    all_gather x1, blocking collectives, on_device(): lax.all_gather(bc_grad, 'tensor', axis=0).astype(f32)  10.7 us
    gather x1, local copies, waits for them, and re-layouts, on_device(): jnp.take(head_gathered, head_owner, axis=0, mode='clip')  9.86 us
  transfers between devices with their start and end apart: 8, of which 6 were waited for; matrix products, arithmetic and copies ran while one was open for 10% of the time, Pallas kernels for 0%

profile of v1, /device:TPU:1, one launch (start us, length us, event | category | flops | bytes accessed | tf_op | source)
XLA Modules:
  0.0 482.8 jit_solution(11957001899699953825)
XLA Ops:
  7.2 1.2 slice.18
  9.8 1.1 copy.20
  12.0 1.2 copy.19
  15.4 6.7 %convolution_convert_fusion = bf16[2560,2560]{1,0:T(8,128)(2,1)} fusion(bf16[256,2560]{0,1:T(8,128)(2,1)S(1)} %bitcast.111, bf16[128,2560]{1,0:T(8,128)(2,1)S(1)} %copy-done.4, bf16[128,2560]{1,0:T(8,128)(2,1)S(1)} %copy-done), kind=kOutput, calls=%fused_computation.1 | convolution fusion | flops 3364618240 | bytes 15728640 | tf_op jit(solution)/shard_map/dot_general | solution.py:85
  22.2 107.0 %reduce-scatter.2.cloned.1.call-done = bf16[80,2560]{1,0:T(8,128)(2,1)} async-done(((bf16[2560,2560]{1,0:T(8,128)(2,1)}), bf16[80,2560]{1,0:T(8,128)(2,1)}) %reduce-scatter.2.cloned.1.call-update) | async-done | bytes 409616 | tf_op jit(solution)/shard_map/reduce_scatter | solution.py:86
  129.2 1.1 bitcast_add_fusion
  145.2 1.4 fusion.3
  146.7 10.7 %all-gather.2 = bf16[512,256]{1,0:T(8,128)(2,1)S(1)} all-gather(bf16[128,256]{1,0:T(8,128)(2,1)S(1)} %copy-done.5), channel_id=4, replica_groups=mesh['dp'=32,'tensor'=4] {'tensor'}, dimensions={0}, use_global_device_ids=true | all-gather | bytes 327680 | tf_op jit(solution)/shard_map/all_gather | solution.py:54
  157.4 1.2 fusion.46
  158.7 4.7 collective-permute-start
  163.3 5.0 %collective-permute-done = f32[256,2560]{1,0:T(8,128)S(1)} collective-permute-done((f32[256,2560]{1,0:T(8,128)S(1)}, f32[256,2560]{1,0:T(8,128)S(1)}, u32[]{:S(2)}, u32[]{:S(2)}) %collective-permute-start) | collective-permute-done | bytes 2621472 | tf_op jit(solution)/shard_map/ppermute | solution.py:64
  169.1 81.1 %collective-permute-done.1 = f32[256,2560]{1,0:T(8,128)S(1)} collective-permute-done((f32[256,2560]{1,0:T(8,128)S(1)}, f32[256,2560]{1,0:T(8,128)S(1)}, u32[]{:S(2)}, u32[]{:S(2)}) %collective-permute-start.1) | collective-permute-done | bytes 2621472 | tf_op jit(solution)/shard_map/ppermute | solution.py:64
  250.5 1.9 collective-permute-start.2
  252.4 61.6 %collective-permute-done.2 = f32[256,2560]{1,0:T(8,128)S(1)} collective-permute-done((f32[256,2560]{1,0:T(8,128)S(1)}, f32[256,2560]{1,0:T(8,128)S(1)}, u32[]{:S(2)}, u32[]{:S(2)}) %collective-permute-start.2) | collective-permute-done | bytes 2621472 | tf_op jit(solution)/shard_map/ppermute | solution.py:64
  314.3 1.2 collective-permute-start.3
  315.6 55.8 %collective-permute-done.3 = f32[256,2560]{1,0:T(8,128)S(1)} collective-permute-done((f32[256,2560]{1,0:T(8,128)S(1)}, f32[256,2560]{1,0:T(8,128)S(1)}, u32[]{:S(2)}, u32[]{:S(2)}) %collective-permute-start.3) | collective-permute-done | bytes 2621472 | tf_op jit(solution)/shard_map/ppermute | solution.py:64
  371.7 3.6 collective-permute-start.4
  377.3 53.2 %collective-permute-done.4 = f32[256,2560]{1,0:T(8,128)} collective-permute-done((f32[256,2560]{1,0:T(8,128)S(1)}, f32[256,2560]{1,0:T(8,128)}, u32[]{:S(2)}, u32[]{:S(2)}) %collective-permute-start.4) | collective-permute-done | bytes 2621472 | tf_op jit(solution)/shard_map/ppermute | solution.py:64
  430.4 2.0 add.188
  433.2 2.8 fusion.37
  436.3 2.4 fusion.36
  438.7 3.2 fusion.26
  442.2 3.2 convolution_add_fusion.3
  445.4 2.5 fusion.47
  448.2 2.6 convolution_add_fusion.2
  450.7 2.5 fusion.48
  453.5 2.6 convolution_add_fusion.1
  456.2 2.8 fusion.49
  459.2 3.7 fusion.1
  463.0 1.6 copy.25
  464.6 1.5 dynamic-slice_bitcast_fusion
  466.1 9.9 %gather_fusion = bf16[30,64,2560]{2,1,0:T(8,128)(2,1)} fusion(bf16[32,64,2560]{2,1,0:T(8,128)(2,1)} %bitcast.109, s32[1024]{0:T(1024)S(1)} %pad_clamp_fusion), kind=kCustom, calls=%fused_computation | custom fusion | bytes 19660920 | tf_op jit(solution)/shard_map/jit(_take)/gather | solution.py:97
  (79 shorter events, 22.0 us)
Async XLA Ops:
  7.2 122.0 %reduce-scatter.2.cloned.1.call-start = ((), (), s32[]{:S(2)}) async-start(), calls=%async_computation.1 | async-start | bytes 13516800 | tf_op jit(solution)/shard_map/reduce_scatter | solution.py:86
  14.1 1.1 copy-start
  14.1 1.3 copy-start.4
  22.1 107.1 %copy-start.3 = (f32[1,74,2560]{2,0,1:T(1,128)S(1)}, f32[1,74,2560]{2,0,1:T(1,128)}, u32[]{:S(2)}) copy-start(f32[1,74,2560]{2,0,1:T(1,128)} %param.16) | copy-start | bytes 2273284
  22.2 442.5 %all-gather.8.cloned.1.call-start = ((), (), s32[]{:S(2)}) async-start(), calls=%async_computation.3 | async-start | bytes 2703360 | tf_op jit(solution)/shard_map/all_gather | solution.py:94
  136.2 330.0 %all-gather.6.cloned.1.call-start = ((), (), s32[]{:S(2)}) async-start(), calls=%async_computation.2 | async-start | bytes 10813440 | tf_op jit(solution)/shard_map/all_gather | solution.py:90
  142.8 3.8 copy-start.5
  158.7 9.7 %collective-permute-start = (f32[256,2560]{1,0:T(8,128)S(1)}, f32[256,2560]{1,0:T(8,128)S(1)}, u32[]{:S(2)}, u32[]{:S(2)}) collective-permute-start(f32[256,2560]{1,0:T(8,128)S(1)} %fusion.46), channel_id=1, source_target_pairs={{0,4},{4,0},{8,12},{12,8},{16,20},{20,16},{24,28},{28,24},{32,36},... | collective-permute-start | bytes 7864328 | tf_op jit(solution)/shard_map/ppermute | solution.py:64
  168.6 81.6 %collective-permute-start.1 = (f32[256,2560]{1,0:T(8,128)S(1)}, f32[256,2560]{1,0:T(8,128)S(1)}, u32[]{:S(2)}, u32[]{:S(2)}) collective-permute-start(f32[256,2560]{1,0:T(8,128)S(1)} %add.184), channel_id=1, source_target_pairs={{0,8},{4,12},{8,0},{12,4},{16,24},{20,28},{24,16},{28,20},{32,40},... | collective-permute-start | bytes 7864328 | tf_op jit(solution)/shard_map/ppermute | solution.py:64
  250.5 63.5 %collective-permute-start.2 = (f32[256,2560]{1,0:T(8,128)S(1)}, f32[256,2560]{1,0:T(8,128)S(1)}, u32[]{:S(2)}, u32[]{:S(2)}) collective-permute-start(f32[256,2560]{1,0:T(8,128)S(1)} %add.185), channel_id=1, source_target_pairs={{0,16},{4,20},{8,24},{12,28},{16,0},{20,4},{24,8},{28,12},{32,48},... | collective-permute-start | bytes 7864328 | tf_op jit(solution)/shard_map/ppermute | solution.py:64
  314.3 57.1 %collective-permute-start.3 = (f32[256,2560]{1,0:T(8,128)S(1)}, f32[256,2560]{1,0:T(8,128)S(1)}, u32[]{:S(2)}, u32[]{:S(2)}) collective-permute-start(f32[256,2560]{1,0:T(8,128)S(1)} %add.186), channel_id=1, source_target_pairs={{0,32},{4,36},{8,40},{12,44},{16,48},{20,52},{24,56},{28,60},{32,0... | collective-permute-start | bytes 7864328 | tf_op jit(solution)/shard_map/ppermute | solution.py:64
  371.7 58.7 %collective-permute-start.4 = (f32[256,2560]{1,0:T(8,128)S(1)}, f32[256,2560]{1,0:T(8,128)}, u32[]{:S(2)}, u32[]{:S(2)}) collective-permute-start(f32[256,2560]{1,0:T(8,128)S(1)} %add.187), channel_id=1, source_target_pairs={{0,64},{4,68},{8,72},{12,76},{16,80},{20,84},{24,88},{28,92},{32,9... | collective-permute-start | bytes 7864328 | tf_op jit(solution)/shard_map/ppermute | solution.py:64
  377.3 55.2 %copy-start.1 = (f32[2,128,2560]{2,1,0:T(8,128)S(1)}, f32[2,128,2560]{2,1,0:T(8,128)}, u32[]{:S(2)}) copy-start(f32[2,128,2560]{2,1,0:T(8,128)} %param.17) | copy-start | bytes 7864324
  433.2 8.9 %copy-start.2 = (f32[2,128,2560]{2,1,0:T(8,128)}, f32[2,128,2560]{2,1,0:T(8,128)S(1)}, u32[]{:S(2)}) copy-start(f32[2,128,2560]{2,1,0:T(8,128)S(1)} %get-tuple-element.16) | copy-start | bytes 7864324
Sparse Core Ops, SparseCore 0:
  22.3 106.8 reduce-scatter.1
  136.3 47.6 all-gather.7
  186.8 74.6 all-gather.5
